TPU v7x, 32 devices: a whole 2x2x4 slice. The times are simulated.
32 devices in a mesh: pw: 8 (over z, y), band: 4 (over x, core).
Axes of the slice: x: 2, y: 2, z: 4, core: 2. Of those that a mesh axis runs over, the one named last changes fastest.
Arguments:
- psi_block: float32 [2, 8, 256, 128], P(None, 'band', 'pw'), may hold values from -6 to 6
- psi_all: bfloat16 [2, 1024, 256, 128], P(None, 'band', 'pw'), may hold values from -0.0234375 to 0.0234375
- potential: float32 [128, 128, 128], P('pw'), may hold values from -8 to 8
- stick_col: int32 [256], replicated, may hold values from 0 to 16383, as said below
Outputs:
- intersection: float32 [2, 8, 1024], P(None, 'pw', 'band')
- hpsi: float32 [2, 8, 256, 128], P(None, 'band', 'pw')
Inputs may be any that keep to these rules, and one draw needn't show every extreme that they name: `stick_col`: distinct columns of the 128 x 128 plane; column 0 and column 16383 are always among them.
All inputs are finite; a program needn't handle non-finite values.
Results may differ from a plain program's by a relative error of at most 0.0029.
Values may be sent and summed in bfloat16 or wider, within the bound.
No kernel may reach another device: no remote copies, remote signals or barrier semaphores. Data moves between devices by JAX's collectives and lax.ppermute only.
A program may use at most 64 MiB of HBM per device.

v0:
```python
import math
import jax
import jax.numpy as jnp
from jax import lax
from jax.sharding import PartitionSpec as P


def frequency(index, size):
    return jnp.where(index < size // 2, index, index - size)


def kinetic_table(columns, grid_size):
    col_x = frequency(columns // grid_size, grid_size).astype(jnp.float32)
    col_y = frequency(columns % grid_size, grid_size).astype(jnp.float32)
    along = frequency(jnp.arange(grid_size, dtype=jnp.int32), grid_size).astype(jnp.float32)
    plane = col_x * col_x + col_y * col_y
    return 4.0 * (plane[:, None] + along[None, :] * along[None, :]) / float(grid_size * grid_size)


def dft_table(grid_size, sign):
    indices = jnp.arange(grid_size, dtype=jnp.int32)
    products = indices[:, None] * indices[None, :] % grid_size
    angles = 2.0 * math.pi / grid_size * products.astype(jnp.float32)
    cosine = jnp.cos(angles)
    sine = sign * jnp.sin(angles)
    return jnp.stack([jnp.stack([cosine, -sine]), jnp.stack([sine, cosine])])


def per_device(psi_block, psi_all, potential, stick_col):
    local_bands = psi_block.shape[1]
    sticks_dev = psi_block.shape[2]
    grid_size = psi_block.shape[3]
    highest = lax.Precision.HIGHEST
    rank = lax.axis_index("pw")
    pw_count = lax.axis_size("pw")
    band_count = lax.axis_size("band")
    my_columns = lax.dynamic_slice_in_dim(stick_col, rank * sticks_dev, sticks_dev)
    kinetic = kinetic_table(my_columns, grid_size)
    inverse = dft_table(grid_size, 1.0)
    forward = dft_table(grid_size, -1.0)
    cosine = inverse[0, 0]
    sine = inverse[1, 0]
    grid_iota = jnp.arange(grid_size, dtype=jnp.int32)
    col_x = stick_col // grid_size
    col_y = stick_col % grid_size
    phase_angles = (
        2.0
        * math.pi
        / grid_size
        * (grid_iota[:, None] * col_y[None, :] % grid_size).astype(jnp.float32)
    )
    phase_cos = jnp.cos(phase_angles)
    phase_sin = jnp.sin(phase_angles)
    place_rows = (col_x[:, None] == grid_iota[None, :]).astype(jnp.float32)
    pick_rows = (grid_iota[:, None] == col_x[None, :]).astype(jnp.float32)
    turned_pot = (jnp.transpose(potential, (0, 2, 1)) / float(grid_size**3))[None]

    def mult(left, right):
        return jnp.dot(left, right, precision=highest, preferred_element_type=jnp.float32)

    all_re = psi_all[0].reshape(psi_all.shape[1], -1)
    all_im = psi_all[1].reshape(psi_all.shape[1], -1)
    dims = (((1,), (1,)), ((), ()))
    group_count = local_bands // 2
    z_lines = jnp.einsum("dcvu,cbsu->bvds", inverse, psi_block, precision=highest)
    planes_in = lax.all_to_all(z_lines, "pw", split_axis=1, concat_axis=3, tiled=True)
    val_re = planes_in[:, :, 0, None, :]
    val_im = planes_in[:, :, 1, None, :]
    spread_re = val_re * phase_cos - val_im * phase_sin
    spread_im = val_re * phase_sin + val_im * phase_cos
    rows_re = mult(spread_re, place_rows)
    rows_im = mult(spread_im, place_rows)
    wave_re = (mult(rows_re, cosine) - mult(rows_im, sine)) * turned_pot
    wave_im = (mult(rows_re, sine) + mult(rows_im, cosine)) * turned_pot
    back_re = mult(wave_re, cosine) + mult(wave_im, sine)
    back_im = mult(wave_im, cosine) - mult(wave_re, sine)
    sel_re = mult(back_re, pick_rows)
    sel_im = mult(back_im, pick_rows)
    picked_re = jnp.sum(sel_re * phase_cos + sel_im * phase_sin, axis=2)
    picked_im = jnp.sum(sel_im * phase_cos - sel_re * phase_sin, axis=2)
    picked = jnp.stack([picked_re, picked_im], axis=2)
    sticks_back = lax.all_to_all(picked, "pw", split_axis=3, concat_axis=1, tiled=True)
    vpsi = jnp.einsum("dcvu,bucs->dbsv", forward, sticks_back, precision=highest)
    applied = kinetic[None, None] * psi_block + vpsi
    lowered = applied.astype(jnp.bfloat16)
    gathered = lax.all_gather(lowered, "band", axis=1, tiled=True)
    h_re = gathered[0].reshape(gathered.shape[1], -1)
    h_im = gathered[1].reshape(gathered.shape[1], -1)
    real_part = lax.dot_general(
        h_re, all_re, dims, preferred_element_type=jnp.float32
    ) + lax.dot_general(h_im, all_im, dims, preferred_element_type=jnp.float32)
    imag_part = lax.dot_general(
        h_re, all_im, dims, preferred_element_type=jnp.float32
    ) - lax.dot_general(h_im, all_re, dims, preferred_element_type=jnp.float32)
    partials = [jnp.stack([real_part, imag_part])]
    stacked = jnp.stack(partials, axis=1)
    stacked = stacked.reshape(2, group_count, band_count, 2, stacked.shape[-1])
    partial_value = jnp.transpose(stacked, (0, 2, 1, 3, 4)).reshape(
        2, band_count * local_bands, stacked.shape[-1]
    )
    summed = lax.psum(partial_value, "pw")
    cols_dev = partial_value.shape[1] // pw_count
    intersection = lax.dynamic_slice_in_dim(summed, rank * cols_dev, cols_dev, 1)
    return (intersection, applied)


def solution(mesh):
    return jax.shard_map(
        per_device,
        mesh=mesh,
        in_specs=(
            P(None, "band", "pw", None),
            P(None, "band", "pw", None),
            P("pw", None, None),
            P(),
        ),
        out_specs=(P(None, "pw", "band"), P(None, "band", "pw", None)),
        check_vma=False,
    )
```

profile of v0, /device:TPU:0, one launch (start us, length us, event | category | flops | bytes accessed | tf_op | source)
XLA Modules:
  0.0 115.9 jit_solution(15763958665738720233)
XLA Ops:
  0.6 0.3 fusion.76
  0.9 0.3 fusion.74
  1.2 0.3 broadcast_multiply_fusion
  1.5 0.7 fusion.40
  2.2 1.2 %convolution_bitcast_fusion = f32[2,128,2,32]{1,3,0,2:T(8,128)S(1)} fusion(f32[1,2,128,128]{3,2,1,0:T(8,128)S(1)} %get-tuple-element.20, f32[1,2,128,128]{3,2,1,0:T(8,128)S(1)} %get-tuple-element.21, f32[2,2,32,128]{3,2,1,0:T(8,128)} %param.4), kind=kOutput, calls=%fused_computation.30 | convolution fusion | flops 50397184 | bytes 393216 | tf_op jit(solution)/shard_map/dcvu,cbsu->bvds/dot_general | solution.py:65
  3.4 0.2 copy.63
  3.6 0.9 reshape.230
  4.5 7.3 %all-to-all-start = ((f32[8,1,2048]{2,1,0:T(1,128)}), f32[8,1,2048]{2,1,0:T(1,128)}, u32[]{:S(2)}, u32[]{:S(2)}) async-start(f32[8,1,2048]{2,1,0:T(1,128)} %reshape.230), calls=%async_computation | async-start | bytes 131072 | tf_op jit(solution)/shard_map/all_to_all | solution.py:66
  11.8 1.2 %fusion.62 = (f32[128,256]{1,0:T(8,128)S(1)}, f32[128,256]{1,0:T(8,128)}) fusion(s32[256]{0:T(256)S(1)} %get-tuple-element.25), kind=kLoop, calls=%fused_computation.86 | loop fusion | flops 458752 | bytes 263168 | tf_op jit(solution)/shard_map/cos | solution.py:52
  13.0 1.1 multiply_bitcast_fusion
  14.1 4.3 %fusion.86 = (bf16[1,256,32,128]{3,2,1,0:T(8,128)(2,1)S(1)}, bf16[1,256,32,128]{3,2,1,0:T(8,128)(2,1)}) fusion(bf16[2,256,32,128]{3,2,1,0:T(8,128)(2,1)} %param.5), kind=kLoop, calls=%fused_computation.131 | loop fusion | bytes 8388608 | tf_op jit(solution)/shard_map/slice | solution.py:61
  18.4 1.6 %copy.66 = f32[16,128,128]{2,1,0:T(8,128)S(1)} copy(f32[16,128,128]{1,2,0:T(8,128)} %multiply_bitcast_fusion) | data formatting | bytes 2097152 | tf_op jit(solution)/shard_map/div | solution.py:56
  20.0 0.1 fusion.79
  20.1 0.5 broadcast.384
  20.6 2.3 %reduce = f32[8,2048]{1,0:T(8,128)} reduce(f32[8,1,2048]{2,1,0:T(1,128)} %all-to-all-done, f32[]{:T(128)} %broadcast.384), dimensions={1}, to_apply=%all_to_all.26.reduce_sub_computation | reduce | bytes 131076 | tf_op jit(solution)/shard_map/all_to_all | solution.py:66
  22.8 1.8 %reshape.231 = f32[128,2,2,32]{3,2,1,0:T(2,128)} reshape(f32[8,2048]{1,0:T(8,128)} %reduce) | data formatting | bytes 131072
  24.6 1.0 copy.64
  25.6 0.8 copy.65
  26.4 1.7 %all_to_all.29 = f32[2,16,2,256]{3,1,2,0:T(8,128)} reshape(f32[2,16,2,8,32]{4,3,1,2,0:T(8,128)} %copy.65) | data formatting | bytes 131072 | tf_op jit(solution)/shard_map/all_to_all | solution.py:66
  28.1 0.8 slice_bitcast_fusion.11
  28.9 3.3 %fusion = f32[2,16,128,128]{3,2,1,0:T(8,128)S(1)} fusion(f32[128,256]{1,0:T(8,128)} %get-tuple-element.27, f32[2,16,256]{2,1,0:T(8,128)S(1)} %get-tuple-element.23, f32[128,256]{1,0:T(8,128)S(1)} %get-tuple-element.26, f32[2,16,256]{2,1,0:T(8,128)S(1)} %get-tuple-element.22, s32[256]{0:T(256)S(1)} %get-tuple-element.24), kind=kOutput, calls=%fused_computation.2 | convolution fusion | flops 1613791232 | bytes 2425856 | tf_op jit(solution)/shard_map/dot_general | solution.py:59
  32.3 2.5 %fusion.4 = f32[2,16,128,128]{3,2,1,0:T(8,128)S(1)} fusion(f32[128,256]{1,0:T(8,128)S(1)} %copy-done.1, f32[2,16,256]{2,1,0:T(8,128)S(1)} %get-tuple-element.23, f32[128,256]{1,0:T(8,128)S(1)} %get-tuple-element.26, f32[2,16,256]{2,1,0:T(8,128)S(1)} %get-tuple-element.22, s32[256]{0:T(256)S(1)} %get-tuple-element.24), kind=kOutput, calls=%fused_computation.6 | convolution fusion | flops 1613791232 | bytes 2425856 | tf_op jit(solution)/shard_map/dot_general | solution.py:59
  34.7 1.9 %fusion.72 = f32[2,16,128,128]{3,2,1,0:T(8,128)S(1)} fusion(f32[2,16,128,128]{3,2,1,0:T(8,128)S(1)} %fusion.4, f32[1,2,128,128]{3,2,1,0:T(8,128)S(1)} %get-tuple-element.20), kind=kOutput, calls=%fused_computation.96 | convolution fusion | flops 805306368 | bytes 4259840 | tf_op jit(solution)/shard_map/dot_general | solution.py:59
  36.6 1.8 %fusion.69 = f32[2,16,128,128]{3,2,1,0:T(8,128)S(1)} fusion(f32[2,16,128,128]{3,2,1,0:T(8,128)S(1)} %fusion.4, f32[1,2,128,128]{3,2,1,0:T(8,128)S(1)} %get-tuple-element.21), kind=kOutput, calls=%fused_computation.93 | convolution fusion | flops 805306368 | bytes 4259840 | tf_op jit(solution)/shard_map/dot_general | solution.py:59
  38.4 2.0 %subtract_multiply_fusion = f32[2,16,128,128]{3,2,1,0:T(8,128)S(1)} fusion(f32[2,16,128,128]{3,2,1,0:T(8,128)S(1)} %fusion.69, f32[2,16,128,128]{3,2,1,0:T(8,128)S(1)} %fusion, f32[16,128,128]{2,1,0:T(8,128)S(1)} %copy.66, f32[1,2,128,128]{3,2,1,0:T(8,128)S(1)} %get-tuple-element.20), kind=kOutput, calls=%fused_computation.17 | convolution fusion | flops 806354944 | bytes 7405568 | tf_op jit(solution)/shard_map/dot_general | solution.py:59
  40.4 1.8 %fusion.70 = f32[2,16,128,128]{3,2,1,0:T(8,128)S(1)} fusion(f32[2,16,128,128]{3,2,1,0:T(8,128)S(1)} %subtract_multiply_fusion, f32[1,2,128,128]{3,2,1,0:T(8,128)S(1)} %get-tuple-element.20), kind=kOutput, calls=%fused_computation.94 | convolution fusion | flops 805306368 | bytes 4259840 | tf_op jit(solution)/shard_map/dot_general | solution.py:59
  42.2 1.8 %fusion.68 = f32[2,16,128,128]{3,2,1,0:T(8,128)S(1)} fusion(f32[2,16,128,128]{3,2,1,0:T(8,128)S(1)} %subtract_multiply_fusion, f32[1,2,128,128]{3,2,1,0:T(8,128)S(1)} %get-tuple-element.21), kind=kOutput, calls=%fused_computation.92 | convolution fusion | flops 805306368 | bytes 4259840 | tf_op jit(solution)/shard_map/dot_general | solution.py:59
  44.0 1.9 %add_multiply_fusion = f32[2,16,128,128]{3,2,1,0:T(8,128)S(1)} fusion(f32[2,16,128,128]{3,2,1,0:T(8,128)S(1)} %fusion.72, f32[2,16,128,128]{3,2,1,0:T(8,128)S(1)} %fusion, f32[16,128,128]{2,1,0:T(8,128)S(1)} %copy.66, f32[1,2,128,128]{3,2,1,0:T(8,128)S(1)} %get-tuple-element.21), kind=kOutput, calls=%fused_computation.16 | convolution fusion | flops 806354944 | bytes 7405568 | tf_op jit(solution)/shard_map/dot_general | solution.py:59
  46.0 1.8 %fusion.67 = f32[2,16,128,128]{3,2,1,0:T(8,128)S(1)} fusion(f32[2,16,128,128]{3,2,1,0:T(8,128)S(1)} %add_multiply_fusion, f32[1,2,128,128]{3,2,1,0:T(8,128)S(1)} %get-tuple-element.21), kind=kOutput, calls=%fused_computation.91 | convolution fusion | flops 805306368 | bytes 4259840 | tf_op jit(solution)/shard_map/dot_general | solution.py:59
  47.7 1.8 %fusion.71 = f32[2,16,128,128]{3,2,1,0:T(8,128)S(1)} fusion(f32[2,16,128,128]{3,2,1,0:T(8,128)S(1)} %add_multiply_fusion, f32[1,2,128,128]{3,2,1,0:T(8,128)S(1)} %get-tuple-element.20), kind=kOutput, calls=%fused_computation.95 | convolution fusion | flops 805306368 | bytes 4259840 | tf_op jit(solution)/shard_map/dot_general | solution.py:59
  49.6 1.8 %fusion.10 = f32[2,16,128,256]{3,2,1,0:T(8,128)S(1)} fusion(f32[2,16,128,128]{3,2,1,0:T(8,128)S(1)} %fusion.68, f32[2,16,128,128]{3,2,1,0:T(8,128)S(1)} %fusion.71, s32[256]{0:T(256)S(1)} %get-tuple-element.24), kind=kOutput, calls=%fused_computation.14 | convolution fusion | flops 1611169792 | bytes 8389632 | tf_op jit(solution)/shard_map/dot_general | solution.py:59
  51.4 2.8 %add_reduce_fusion = (f32[2,16,256]{2,1,0:T(8,128)S(1)}, f32[2,16,256]{2,1,0:T(8,128)S(1)}) fusion(f32[2,16,128,256]{3,2,1,0:T(8,128)S(1)} %fusion.10, f32[128,256]{1,0:T(8,128)S(1)} %copy-done.1, f32[128,256]{1,0:T(8,128)S(1)} %get-tuple-element.26, s32[256]{0:T(256)S(1)} %get-tuple-element.24, f32[2,16,128,128]{3,2,1,0:T(8,128)S(1)} %fusion.67, ...), kind=kOutput, calls=%fused_computation.1 | convolution fusion | flops 1619542016 | bytes 8717312 | tf_op jit(solution)/shard_map/dot_general | solution.py:59
  54.2 0.3 copy.67
  54.5 1.4 %reshape.232 = f32[8,1,2048]{2,1,0:T(1,128)} reshape(f32[256,2,2,16]{3,2,1,0:T(2,128)S(1)} %bitcast.156) | data formatting | bytes 131072
  55.9 6.0 %all-to-all-start.1 = ((f32[8,1,2048]{2,1,0:T(1,128)}), f32[8,1,2048]{2,1,0:T(1,128)S(1)}, u32[]{:S(2)}, u32[]{:S(2)}) async-start(f32[8,1,2048]{2,1,0:T(1,128)} %reshape.232), calls=%async_computation.1 | async-start | bytes 131072 | tf_op jit(solution)/shard_map/all_to_all | solution.py:82
  62.0 6.8 %all-to-all-done.1 = f32[8,1,2048]{2,1,0:T(1,128)S(1)} async-done(((f32[8,1,2048]{2,1,0:T(1,128)}), f32[8,1,2048]{2,1,0:T(1,128)S(1)}, u32[]{:S(2)}, u32[]{:S(2)}) %all-to-all-start.1) | async-done | bytes 65568 | tf_op jit(solution)/shard_map/all_to_all | solution.py:82
  68.8 0.8 reduce.1
  69.6 0.7 reshape.233
  70.3 0.3 copy.85
  70.7 0.6 fusion.88
  71.2 0.6 copy.75
  71.9 5.4 %all_gather.3 = bf16[2,8,32,128]{3,2,0,1:T(8,128)(2,1)S(1)} all-gather(bf16[2,2,32,128]{3,2,0,1:T(8,128)(2,1)S(1)} %get-tuple-element.28), channel_id=1, replica_groups=mesh['pw'=8,'band'=4] {'band'}, dimensions={1}, use_global_device_ids=true | all-gather | bytes 163840 | tf_op jit(solution)/shard_map/all_gather | solution.py:86
  77.3 2.3 %fusion.26 = f32[8,256]{1,0:T(8,128)S(1)} fusion(bf16[1,256,32,128]{3,2,1,0:T(8,128)(2,1)} %get-tuple-element.15, bf16[1,8,32,128]{3,2,0,1:T(8,128)(2,1)S(1)} %get-tuple-element.17), kind=kOutput, calls=%fused_computation.34 | convolution fusion | flops 16777216 | bytes 2170880 | tf_op jit(solution)/shard_map/dot_general | solution.py:92
  79.6 0.7 fusion.25
  80.3 0.7 fusion.30
  81.0 0.7 fusion.32
  81.7 33.7 %psum.7 = f32[2,8,256]{2,1,0:T(8,128)S(1)} all-reduce(f32[2,8,256]{2,1,0:T(8,128)S(1)} %pad_maximum_fusion.5), channel_id=1, replica_groups=mesh['pw'=8,'band'=4] {'pw'}, use_global_device_ids=true, to_apply=%region_2.3 | all-reduce | flops 4096 | bytes 32768 | tf_op jit(solution)/shard_map/psum | solution.py:101
  115.3 0.6 constant_dynamic-slice_fusion
  (21 shorter events, 0.1 us)
Async XLA Ops:
  0.6 11.2 %copy-start.6 = (s32[256]{0:T(256)S(1)}, s32[256]{0:T(256)}, u32[]{:S(2)}) copy-start(s32[256]{0:T(256)} %param.7) | copy-start | bytes 3076
  0.6 12.4 %copy-start.2 = (f32[16,128,128]{2,1,0:T(8,128)S(1)}, f32[16,128,128]{2,1,0:T(8,128)}, u32[]{:S(2)}) copy-start(f32[16,128,128]{2,1,0:T(8,128)} %param.6) | copy-start | bytes 3145732
  4.5 15.5 %all-to-all-start = ((f32[8,1,2048]{2,1,0:T(1,128)}), f32[8,1,2048]{2,1,0:T(1,128)}, u32[]{:S(2)}, u32[]{:S(2)}) async-start(f32[8,1,2048]{2,1,0:T(1,128)} %reshape.230), calls=%async_computation | async-start | bytes 131072 | tf_op jit(solution)/shard_map/all_to_all | solution.py:66
  28.1 4.2 %copy-start.1 = (f32[128,256]{1,0:T(8,128)S(1)}, f32[128,256]{1,0:T(8,128)}, u32[]{:S(2)}) copy-start(f32[128,256]{1,0:T(8,128)} %get-tuple-element.27) | copy-start | bytes 393220
  54.2 16.5 %copy-start.3 = (f32[1,2,128,128]{3,2,1,0:T(8,128)S(1)}, f32[1,2,128,128]{3,2,1,0:T(8,128)}, u32[]{:S(2)}) copy-start(f32[1,2,128,128]{3,2,1,0:T(8,128)} %get-tuple-element.18) | copy-start | bytes 393220
  54.2 16.5 %copy-start.4 = (f32[1,2,128,128]{3,2,1,0:T(8,128)S(1)}, f32[1,2,128,128]{3,2,1,0:T(8,128)}, u32[]{:S(2)}) copy-start(f32[1,2,128,128]{3,2,1,0:T(8,128)} %get-tuple-element.19) | copy-start | bytes 393220
  54.2 16.5 %copy-start.5 = (f32[2,2,32,128]{3,2,1,0:T(8,128)S(1)}, f32[2,2,32,128]{3,2,1,0:T(8,128)}, u32[]{:S(2)}) copy-start(f32[2,2,32,128]{3,2,1,0:T(8,128)} %param.4) | copy-start | bytes 196612
  55.9 12.9 %all-to-all-start.1 = ((f32[8,1,2048]{2,1,0:T(1,128)}), f32[8,1,2048]{2,1,0:T(1,128)S(1)}, u32[]{:S(2)}, u32[]{:S(2)}) async-start(f32[8,1,2048]{2,1,0:T(1,128)} %reshape.232), calls=%async_computation.1 | async-start | bytes 131072 | tf_op jit(solution)/shard_map/all_to_all | solution.py:82
  70.6 9.0 %copy-start = (bf16[1,256,32,128]{3,2,1,0:T(8,128)(2,1)S(1)}, bf16[1,256,32,128]{3,2,1,0:T(8,128)(2,1)}, u32[]{:S(2)}) copy-start(bf16[1,256,32,128]{3,2,1,0:T(8,128)(2,1)} %get-tuple-element.15) | copy-start | bytes 6291460
where the time goes:
time: 117 us; the launch traced here: 116 us
  blocking collectives  39.1 us (33%)
  matrix products  31.3 us (27%)
  local copies, waits for them, and re-layouts  17.5 us (15%)
  starting transfers between devices  13.3 us (11%)
  other arithmetic  7.07 us (6%)
  waiting for transfers between devices  6.84 us (6%)
    psum x1, blocking collectives, per_device(): summed = lax.psum(partial_value, 'pw')  33.7 us
    dot_general x12, matrix products, mult(): jnp.dot(left, right, precision=highest, preferred_element_type=jnp.float32)  25.2 us
    all_to_all x1, starting transfers between devices, per_device(): lax.all_to_all(z_lines, 'pw', split_axis=1, concat_axis=3, tiled=True)  7.28 us
    all_to_all x1, waiting for transfers between devices, per_device(): lax.all_to_all(picked, 'pw', split_axis=3, concat_axis=1, tiled=True)  6.83 us
    all_to_all x1, starting transfers between devices, per_device(): lax.all_to_all(picked, 'pw', split_axis=3, concat_axis=1, tiled=True)  5.99 us
    unnamed x19, local copies, waits for them, and re-layouts  5.42 us
    all_gather x1, blocking collectives, per_device(): gathered = lax.all_gather(lowered, 'band', axis=1, tiled=True)  5.41 us
    slice x1, local copies, waits for them, and re-layouts, per_device(): all_re = psi_all[0].reshape(psi_all.shape[1], -1)  4.29 us
  transfers between devices with their start and end apart: 2, of which 1 were waited for; matrix products, arithmetic and copies ran while one was open for 7% of the time, Pallas kernels for 0%

commit v1 on v0

--- a/solution.py
+++ b/solution.py
@@ -83,7 +83,12 @@
     vpsi = jnp.einsum("dcvu,bucs->dbsv", forward, sticks_back, precision=highest)
     applied = kinetic[None, None] * psi_block + vpsi
     lowered = applied.astype(jnp.bfloat16)
-    gathered = lax.all_gather(lowered, "band", axis=1, tiled=True)
+    ring = [lowered]
+    for hop in range(3):
+        ring.append(lax.ppermute(ring[-1], "band", [(dev, (dev + 1) % 4) for dev in range(4)]))
+    gathered = jnp.roll(
+        jnp.concatenate(ring[::-1], axis=1), (lax.axis_index("band") + 1) * ring[0].shape[1], axis=1
+    )
     h_re = gathered[0].reshape(gathered.shape[1], -1)
     h_im = gathered[1].reshape(gathered.shape[1], -1)
     real_part = lax.dot_general(

time: 117 us -> 109 us (0.932); the launches traced: 116 us -> 109 us
  waiting for transfers between devices: 6.84 us -> 19.2 us
  local copies, waits for them, and re-layouts: 17.5 us -> 10.7 us
  blocking collectives: 39.1 us -> 33.7 us
  other arithmetic: 7.07 us -> 3.25 us
  starting transfers between devices: 13.3 us -> 10.7 us
    ppermute x0 -> x3, waiting for transfers between devices: none -> 6.67 us  [per_device(): lax.ppermute(ring[-1], 'band', [(dev, (dev + 1) % 4) for dev in range(4)])]
    all_to_all x1, waiting for transfers between devices: 0.01 us -> 5.79 us  [per_device(): lax.all_to_all(z_lines, 'pw', split_axis=1, concat_axis=3, tiled=True)]
    all_gather x1 -> x0, blocking collectives: 5.41 us -> none  [per_device(): gathered = lax.all_gather(lowered, 'band', axis=1, tiled=True)]
    all_to_all x4, local copies, waits for them, and re-layouts: 3.97 us -> 0.74 us  [per_device(): lax.all_to_all(z_lines, 'pw', split_axis=1, concat_axis=3, tiled=True)]
    all_to_all x1, starting transfers between devices: 5.99 us -> 3.35 us  [per_device(): lax.all_to_all(picked, 'pw', split_axis=3, concat_axis=1, tiled=True)]
    unnamed x19 -> x20, local copies, waits for them, and re-layouts: 5.42 us -> 3.93 us
    all_to_all x1, other arithmetic: 2.27 us -> 0.8 us  [per_device(): lax.all_to_all(z_lines, 'pw', split_axis=1, concat_axis=3, tiled=True)]
    div x1, local copies, waits for them, and re-layouts: 1.55 us -> 0.33 us  [per_device(): jnp.transpose(potential, (0, 2, 1)) / float(grid_size ** 3)]
  transfers between devices with their start and end apart: 2 -> 5, of which waited for: 1 -> 4; matrix products, arithmetic and copies ran while one was open for 7% -> 6% of each run, Pallas kernels for 0% -> 0%
where the time goes in v1:
time: 109 us
  blocking collectives  33.7 us (31%)
  matrix products  30.6 us (28%)
  waiting for transfers between devices  19.2 us (18%)
  local copies, waits for them, and re-layouts  10.7 us (10%)
  starting transfers between devices  10.7 us (10%)
  other arithmetic  3.25 us (3%)
    psum x1, blocking collectives, per_device(): summed = lax.psum(partial_value, 'pw')  33.7 us
    dot_general x12, matrix products, mult(): jnp.dot(left, right, precision=highest, preferred_element_type=jnp.float32)  24.4 us
    all_to_all x1, starting transfers between devices, per_device(): lax.all_to_all(z_lines, 'pw', split_axis=1, concat_axis=3, tiled=True)  7.28 us
    all_to_all x1, waiting for transfers between devices, per_device(): lax.all_to_all(picked, 'pw', split_axis=3, concat_axis=1, tiled=True)  6.77 us
    ppermute x3, waiting for transfers between devices, per_device(): lax.ppermute(ring[-1], 'band', [(dev, (dev + 1) % 4) for dev in range(4)])  6.67 us
    all_to_all x1, waiting for transfers between devices, per_device(): lax.all_to_all(z_lines, 'pw', split_axis=1, concat_axis=3, tiled=True)  5.79 us
    slice x1, local copies, waits for them, and re-layouts, per_device(): all_re = psi_all[0].reshape(psi_all.shape[1], -1)  4.3 us
    unnamed x20, local copies, waits for them, and re-layouts  3.93 us
  transfers between devices with their start and end apart: 5, of which 4 were waited for; matrix products, arithmetic and copies ran while one was open for 6% of the time, Pallas kernels for 0%

profile of v1, /device:TPU:0, one launch (start us, length us, event | category | flops | bytes accessed | tf_op | source)
XLA Modules:
  0.0 109.1 jit_solution(3867865892417051587)
XLA Ops:
  0.6 0.3 fusion.80
  0.9 0.3 fusion.78
  1.2 0.3 broadcast_multiply_fusion
  1.5 1.2 %convolution_bitcast_fusion = f32[2,128,2,32]{1,3,0,2:T(8,128)S(1)} fusion(f32[1,2,128,128]{3,2,1,0:T(8,128)S(1)} %get-tuple-element.20, f32[1,2,128,128]{3,2,1,0:T(8,128)S(1)} %get-tuple-element.21, f32[2,2,32,128]{3,2,1,0:T(8,128)} %param.4), kind=kOutput, calls=%fused_computation.30 | convolution fusion | flops 50397184 | bytes 393216 | tf_op jit(solution)/shard_map/dcvu,cbsu->bvds/dot_general | solution.py:65
  2.7 0.2 copy.67
  2.9 0.9 reshape.230
  3.8 7.3 %all-to-all-start = ((f32[8,1,2048]{2,1,0:T(1,128)}), f32[8,1,2048]{2,1,0:T(1,128)S(1)}, u32[]{:S(2)}, u32[]{:S(2)}) async-start(f32[8,1,2048]{2,1,0:T(1,128)} %reshape.230), calls=%async_computation | async-start | bytes 131072 | tf_op jit(solution)/shard_map/all_to_all | solution.py:66
  11.1 0.5 fusion.62
  11.7 0.1 multiply_bitcast_fusion
  11.8 0.3 copy.70
  12.1 0.1 fusion.83
  12.2 5.8 %all-to-all-done = f32[8,1,2048]{2,1,0:T(1,128)S(1)} async-done(((f32[8,1,2048]{2,1,0:T(1,128)}), f32[8,1,2048]{2,1,0:T(1,128)S(1)}, u32[]{:S(2)}, u32[]{:S(2)}) %all-to-all-start) | async-done | bytes 65568 | tf_op jit(solution)/shard_map/all_to_all | solution.py:66
  18.0 0.5 broadcast.393
  18.5 0.8 reduce
  19.3 0.2 reshape.231
  19.6 0.1 copy.69
  19.7 0.1 all_to_all.29
  19.8 2.4 %fusion = f32[2,16,128,128]{3,2,1,0:T(8,128)S(1)} fusion(f32[128,256]{1,0:T(8,128)S(1)} %get-tuple-element.27, f32[2,16,256]{2,1,0:T(8,128)S(1)} %get-tuple-element.23, f32[128,256]{1,0:T(8,128)S(1)} %get-tuple-element.26, f32[2,16,256]{2,1,0:T(8,128)S(1)} %get-tuple-element.22, s32[256]{0:T(256)S(1)} %get-tuple-element.24), kind=kOutput, calls=%fused_computation.2 | convolution fusion | flops 1613791232 | bytes 2425856 | tf_op jit(solution)/shard_map/dot_general | solution.py:59
  22.3 2.4 %fusion.4 = f32[2,16,128,128]{3,2,1,0:T(8,128)S(1)} fusion(f32[128,256]{1,0:T(8,128)S(1)} %get-tuple-element.27, f32[2,16,256]{2,1,0:T(8,128)S(1)} %get-tuple-element.23, f32[128,256]{1,0:T(8,128)S(1)} %get-tuple-element.26, f32[2,16,256]{2,1,0:T(8,128)S(1)} %get-tuple-element.22, s32[256]{0:T(256)S(1)} %get-tuple-element.24), kind=kOutput, calls=%fused_computation.6 | convolution fusion | flops 1613791232 | bytes 2425856 | tf_op jit(solution)/shard_map/dot_general | solution.py:59
  24.7 1.8 %fusion.76 = f32[2,16,128,128]{3,2,1,0:T(8,128)S(1)} fusion(f32[2,16,128,128]{3,2,1,0:T(8,128)S(1)} %fusion.4, f32[1,2,128,128]{3,2,1,0:T(8,128)S(1)} %get-tuple-element.20), kind=kOutput, calls=%fused_computation.100 | convolution fusion | flops 805306368 | bytes 4259840 | tf_op jit(solution)/shard_map/dot_general | solution.py:59
  26.6 1.8 %fusion.73 = f32[2,16,128,128]{3,2,1,0:T(8,128)S(1)} fusion(f32[2,16,128,128]{3,2,1,0:T(8,128)S(1)} %fusion.4, f32[1,2,128,128]{3,2,1,0:T(8,128)S(1)} %get-tuple-element.21), kind=kOutput, calls=%fused_computation.97 | convolution fusion | flops 805306368 | bytes 4259840 | tf_op jit(solution)/shard_map/dot_general | solution.py:59
  28.4 1.9 %subtract_multiply_fusion = f32[2,16,128,128]{3,2,1,0:T(8,128)S(1)} fusion(f32[2,16,128,128]{3,2,1,0:T(8,128)S(1)} %fusion.73, f32[2,16,128,128]{3,2,1,0:T(8,128)S(1)} %fusion, f32[16,128,128]{2,1,0:T(8,128)S(1)} %copy.70, f32[1,2,128,128]{3,2,1,0:T(8,128)S(1)} %get-tuple-element.20), kind=kOutput, calls=%fused_computation.17 | convolution fusion | flops 806354944 | bytes 7405568 | tf_op jit(solution)/shard_map/dot_general | solution.py:59
  30.4 2.0 %fusion.74 = f32[2,16,128,128]{3,2,1,0:T(8,128)S(1)} fusion(f32[2,16,128,128]{3,2,1,0:T(8,128)S(1)} %subtract_multiply_fusion, f32[1,2,128,128]{3,2,1,0:T(8,128)S(1)} %get-tuple-element.20), kind=kOutput, calls=%fused_computation.98 | convolution fusion | flops 805306368 | bytes 4259840 | tf_op jit(solution)/shard_map/dot_general | solution.py:59
  32.4 1.8 %fusion.72 = f32[2,16,128,128]{3,2,1,0:T(8,128)S(1)} fusion(f32[2,16,128,128]{3,2,1,0:T(8,128)S(1)} %subtract_multiply_fusion, f32[1,2,128,128]{3,2,1,0:T(8,128)S(1)} %get-tuple-element.21), kind=kOutput, calls=%fused_computation.96 | convolution fusion | flops 805306368 | bytes 4259840 | tf_op jit(solution)/shard_map/dot_general | solution.py:59
  34.2 1.9 %add_multiply_fusion = f32[2,16,128,128]{3,2,1,0:T(8,128)S(1)} fusion(f32[2,16,128,128]{3,2,1,0:T(8,128)S(1)} %fusion.76, f32[2,16,128,128]{3,2,1,0:T(8,128)S(1)} %fusion, f32[16,128,128]{2,1,0:T(8,128)S(1)} %copy.70, f32[1,2,128,128]{3,2,1,0:T(8,128)S(1)} %get-tuple-element.21), kind=kOutput, calls=%fused_computation.16 | convolution fusion | flops 806354944 | bytes 7405568 | tf_op jit(solution)/shard_map/dot_general | solution.py:59
  36.1 1.8 %fusion.71 = f32[2,16,128,128]{3,2,1,0:T(8,128)S(1)} fusion(f32[2,16,128,128]{3,2,1,0:T(8,128)S(1)} %add_multiply_fusion, f32[1,2,128,128]{3,2,1,0:T(8,128)S(1)} %get-tuple-element.21), kind=kOutput, calls=%fused_computation.95 | convolution fusion | flops 805306368 | bytes 4259840 | tf_op jit(solution)/shard_map/dot_general | solution.py:59
  37.9 1.8 %fusion.75 = f32[2,16,128,128]{3,2,1,0:T(8,128)S(1)} fusion(f32[2,16,128,128]{3,2,1,0:T(8,128)S(1)} %add_multiply_fusion, f32[1,2,128,128]{3,2,1,0:T(8,128)S(1)} %get-tuple-element.20), kind=kOutput, calls=%fused_computation.99 | convolution fusion | flops 805306368 | bytes 4259840 | tf_op jit(solution)/shard_map/dot_general | solution.py:59
  39.8 1.8 %fusion.10 = f32[2,16,128,256]{3,2,1,0:T(8,128)S(1)} fusion(f32[2,16,128,128]{3,2,1,0:T(8,128)S(1)} %fusion.72, f32[2,16,128,128]{3,2,1,0:T(8,128)S(1)} %fusion.75, s32[256]{0:T(256)S(1)} %get-tuple-element.24), kind=kOutput, calls=%fused_computation.14 | convolution fusion | flops 1611169792 | bytes 8389632 | tf_op jit(solution)/shard_map/dot_general | solution.py:59
  41.6 2.8 %add_reduce_fusion = (f32[2,16,256]{2,1,0:T(8,128)S(1)}, f32[2,16,256]{2,1,0:T(8,128)S(1)}) fusion(f32[2,16,128,256]{3,2,1,0:T(8,128)S(1)} %fusion.10, f32[128,256]{1,0:T(8,128)S(1)} %get-tuple-element.27, f32[128,256]{1,0:T(8,128)S(1)} %get-tuple-element.26, s32[256]{0:T(256)S(1)} %get-tuple-element.24, f32[2,16,128,128]{3,2,1,0:T(8,128)S(1)} %fusion.71, ...), kind=kOutput, calls=%fused_computation.1 | convolution fusion | flops 1619542016 | bytes 8717312 | tf_op jit(solution)/shard_map/dot_general | solution.py:59
  44.4 0.3 copy.71
  44.7 1.4 %reshape.232 = f32[8,1,2048]{2,1,0:T(1,128)} reshape(f32[256,2,2,16]{3,2,1,0:T(2,128)S(1)} %bitcast.152) | data formatting | bytes 131072
  46.1 3.4 %all-to-all-start.1 = ((f32[8,1,2048]{2,1,0:T(1,128)}), f32[8,1,2048]{2,1,0:T(1,128)S(1)}, u32[]{:S(2)}, u32[]{:S(2)}) async-start(f32[8,1,2048]{2,1,0:T(1,128)} %reshape.232), calls=%async_computation.1 | async-start | bytes 131072 | tf_op jit(solution)/shard_map/all_to_all | solution.py:82
  49.4 0.1 add_multiply_fusion.1
  49.5 6.8 %all-to-all-done.1 = f32[8,1,2048]{2,1,0:T(1,128)S(1)} async-done(((f32[8,1,2048]{2,1,0:T(1,128)}), f32[8,1,2048]{2,1,0:T(1,128)S(1)}, u32[]{:S(2)}, u32[]{:S(2)}) %all-to-all-start.1) | async-done | bytes 65568 | tf_op jit(solution)/shard_map/all_to_all | solution.py:82
  56.3 0.8 reduce.1
  57.1 0.7 reshape.233
  57.8 0.3 copy.91
  58.1 0.6 fusion.91
  58.8 3.3 %collective-permute-done = bf16[2,2,32,128]{3,2,0,1:T(8,128)(2,1)S(1)} collective-permute-done((bf16[2,2,32,128]{3,2,0,1:T(8,128)(2,1)S(1)}, bf16[2,2,32,128]{3,2,0,1:T(8,128)(2,1)S(1)}, u32[]{:S(2)}, u32[]{:S(2)}) %collective-permute-start) | collective-permute-done | bytes 32800 | tf_op jit(solution)/shard_map/ppermute | solution.py:88
  62.1 3.3 %collective-permute-done.1 = bf16[2,2,32,128]{3,2,0,1:T(8,128)(2,1)S(1)} collective-permute-done((bf16[2,2,32,128]{3,2,0,1:T(8,128)(2,1)S(1)}, bf16[2,2,32,128]{3,2,0,1:T(8,128)(2,1)S(1)}, u32[]{:S(2)}, u32[]{:S(2)}) %collective-permute-start.1) | collective-permute-done | bytes 32800 | tf_op jit(solution)/shard_map/ppermute | solution.py:88
  65.4 4.3 %fusion.90 = (bf16[1,256,32,128]{3,2,1,0:T(8,128)(2,1)S(1)}, bf16[1,256,32,128]{3,2,1,0:T(8,128)(2,1)}) fusion(bf16[2,256,32,128]{3,2,1,0:T(8,128)(2,1)} %param.5), kind=kLoop, calls=%fused_computation.143 | loop fusion | bytes 8388608 | tf_op jit(solution)/shard_map/slice | solution.py:61
  69.7 0.6 copy.81
  70.5 2.3 %fusion.26 = f32[8,256]{1,0:T(8,128)S(1)} fusion(bf16[1,256,32,128]{3,2,1,0:T(8,128)(2,1)} %get-tuple-element.15, bf16[8,32,128]{2,1,0:T(8,128)(2,1)S(1)} %get-tuple-element.17), kind=kOutput, calls=%fused_computation.34 | convolution fusion | flops 16777216 | bytes 2170880 | tf_op jit(solution)/shard_map/dot_general | solution.py:97
  72.8 0.7 fusion.25
  73.5 0.7 fusion.30
  74.2 0.7 fusion.32
  74.9 33.7 %psum.7 = f32[2,8,256]{2,1,0:T(8,128)S(1)} all-reduce(f32[2,8,256]{2,1,0:T(8,128)S(1)} %pad_maximum_fusion.5), channel_id=1, replica_groups=mesh['pw'=8,'band'=4] {'pw'}, use_global_device_ids=true, to_apply=%region_2.3 | all-reduce | flops 4096 | bytes 32768 | tf_op jit(solution)/shard_map/psum | solution.py:106
  108.5 0.6 constant_dynamic-slice_fusion
  (28 shorter events, 0.3 us)
Async XLA Ops:
  0.6 10.5 %copy-start.3 = (s32[256]{0:T(256)S(1)}, s32[256]{0:T(256)}, u32[]{:S(2)}) copy-start(s32[256]{0:T(256)} %param.7) | copy-start | bytes 3076
  0.6 11.0 %copy-start.1 = (f32[16,128,128]{2,1,0:T(8,128)S(1)}, f32[16,128,128]{2,1,0:T(8,128)}, u32[]{:S(2)}) copy-start(f32[16,128,128]{2,1,0:T(8,128)} %param.6) | copy-start | bytes 3145732
  3.8 14.2 %all-to-all-start = ((f32[8,1,2048]{2,1,0:T(1,128)}), f32[8,1,2048]{2,1,0:T(1,128)S(1)}, u32[]{:S(2)}, u32[]{:S(2)}) async-start(f32[8,1,2048]{2,1,0:T(1,128)} %reshape.230), calls=%async_computation | async-start | bytes 131072 | tf_op jit(solution)/shard_map/all_to_all | solution.py:66
  44.4 13.7 %copy-start.2 = (f32[2,2,32,128]{3,2,1,0:T(8,128)S(1)}, f32[2,2,32,128]{3,2,1,0:T(8,128)}, u32[]{:S(2)}) copy-start(f32[2,2,32,128]{3,2,1,0:T(8,128)} %param.4) | copy-start | bytes 196612
  46.1 10.2 %all-to-all-start.1 = ((f32[8,1,2048]{2,1,0:T(1,128)}), f32[8,1,2048]{2,1,0:T(1,128)S(1)}, u32[]{:S(2)}, u32[]{:S(2)}) async-start(f32[8,1,2048]{2,1,0:T(1,128)} %reshape.232), calls=%async_computation.1 | async-start | bytes 131072 | tf_op jit(solution)/shard_map/all_to_all | solution.py:82
  58.7 3.4 %collective-permute-start = (bf16[2,2,32,128]{3,2,0,1:T(8,128)(2,1)S(1)}, bf16[2,2,32,128]{3,2,0,1:T(8,128)(2,1)S(1)}, u32[]{:S(2)}, u32[]{:S(2)}) collective-permute-start(bf16[2,2,32,128]{3,2,0,1:T(8,128)(2,1)S(1)} %get-tuple-element.28), channel_id=1, source_target_pairs={{0,1},{1,2},{2,3},{3,0},{4,5},{5,6},{6,7},{7,4},{8,9},{9,10},{10,1... | collective-permute-start | bytes 98312 | tf_op jit(solution)/shard_map/ppermute | solution.py:88
  62.1 3.3 %collective-permute-start.1 = (bf16[2,2,32,128]{3,2,0,1:T(8,128)(2,1)S(1)}, bf16[2,2,32,128]{3,2,0,1:T(8,128)(2,1)S(1)}, u32[]{:S(2)}, u32[]{:S(2)}) collective-permute-start(bf16[2,2,32,128]{3,2,0,1:T(8,128)(2,1)S(1)} %collective-permute-done), channel_id=1, source_target_pairs={{0,1},{1,2},{2,3},{3,0},{4,5},{5,6},{6,7},{7,4},{8,9},{9,10},{10,1... | collective-permute-start | bytes 98312 | tf_op jit(solution)/shard_map/ppermute | solution.py:88
  65.4 4.9 %collective-permute-start.2 = (bf16[2,2,32,128]{3,2,0,1:T(8,128)(2,1)S(1)}, bf16[2,2,32,128]{3,2,0,1:T(8,128)(2,1)S(1)}, u32[]{:S(2)}, u32[]{:S(2)}) collective-permute-start(bf16[2,2,32,128]{3,2,0,1:T(8,128)(2,1)S(1)} %collective-permute-done.1), channel_id=1, source_target_pairs={{0,1},{1,2},{2,3},{3,0},{4,5},{5,6},{6,7},{7,4},{8,9},{9,10},{10,1... | collective-permute-start | bytes 98312 | tf_op jit(solution)/shard_map/ppermute | solution.py:88
  69.7 3.1 %copy-start = (bf16[1,256,32,128]{3,2,1,0:T(8,128)(2,1)S(1)}, bf16[1,256,32,128]{3,2,1,0:T(8,128)(2,1)}, u32[]{:S(2)}) copy-start(bf16[1,256,32,128]{3,2,1,0:T(8,128)(2,1)} %get-tuple-element.15) | copy-start | bytes 6291460
